TPU v7x, 256 devices: a whole 4x4x8 slice. The times are simulated.
256 devices in a mesh: dp: 64 (over x, z_lo, y, core), fsdp: 4 (over z_hi).
Axes of the slice: x: 4, y: 4, z: 8 (z_hi: 4, z_lo: 2; z = z_hi * 2 + z_lo), core: 2. Of those that a mesh axis runs over, the one named last changes fastest.
Arguments:
- bag_ids: int32 [32768, 64, 4], P(('dp', 'fsdp')), may hold values from 0 to 8191
- bag_counts: int32 [32768, 64], P(('dp', 'fsdp')), may hold values from 1 to 4
- emb_table: bfloat16 [8192, 8192], P(None, 'dp'), may hold values from -3 to 3
- cross_down: bfloat16 [8192, 512], P('fsdp'), may hold values from -0.0625 to 0.0625
- cross_up: bfloat16 [512, 8192], P(None, 'fsdp'), may hold values from -0.25 to 0.25
- cross_bias: float32 [8192], replicated, may hold values from -2 to 2
- cotangent: bfloat16 [32768, 8192], P(('dp', 'fsdp')), may hold values from -4 to 4
Outputs:
- table_grad: float32 [8192, 8192], P('fsdp', 'dp')
Inputs may be any that keep to these rules, and one draw needn't show every extreme that they name: `bag_ids`: ids at positions at or past a bag's count are read by no step.
All inputs are finite; a program needn't handle non-finite values.
Results may differ from a plain program's by a relative error of at most 0.0045.
Values may be sent and summed in bfloat16 or wider, within the bound.
No kernel may reach another device: no remote copies, remote signals or barrier semaphores. Data moves between devices by JAX's collectives and lax.ppermute only.
A program may use at most 192 MiB of HBM per device.

v0:
```python
import jax
import jax.numpy as jnp
from jax import lax
from jax.sharding import PartitionSpec as P


def scatter_rows(height, index_rows, grads, table_count, slot_count, embed_width, offset):
    sample_count = index_rows.shape[0]
    local_rows = index_rows.reshape(sample_count, table_count, slot_count) - offset
    inside = (local_rows >= 0) & (local_rows < height)
    table_iota = lax.broadcasted_iota(jnp.int32, local_rows.shape, 1)
    flat_rows = jnp.where(inside, local_rows * table_count + table_iota, height * table_count)
    column_grads = grads.reshape(sample_count, table_count, 1, embed_width).astype(jnp.float32)
    updates = jnp.broadcast_to(column_grads, (sample_count, table_count, slot_count, embed_width))
    target = jnp.zeros((height * table_count, embed_width), jnp.float32)
    target = target.at[flat_rows.reshape(-1)].add(updates.reshape(-1, embed_width), mode="drop")
    return target


def on_device(bag_ids, bag_counts, emb_table, cross_down, cross_up, cross_bias, cotangent):
    row_count, table_count, slot_count = bag_ids.shape
    vocab_rows, col_piece = emb_table.shape
    dp_size = lax.axis_size("dp")
    local_tables = table_count // dp_size
    embed_width = col_piece // local_tables
    slot_iota = lax.broadcasted_iota(jnp.int32, bag_ids.shape, 2)
    live_ids = jnp.where(slot_iota < bag_counts[:, :, None], bag_ids, vocab_rows)
    send_ids = live_ids.reshape(row_count, table_count * slot_count)
    got_ids = lax.all_to_all(send_ids, "dp", split_axis=1, concat_axis=0, tiled=True)
    sample_count = got_ids.shape[0]
    table_iota = lax.broadcasted_iota(jnp.int32, (sample_count, local_tables, slot_count), 1)
    flat_ids = got_ids.reshape(sample_count, local_tables, slot_count) * local_tables + table_iota
    picked = jnp.take(emb_table, flat_ids, axis=0, mode="fill", fill_value=0)
    pooled_local = jnp.sum(picked.astype(jnp.float32), axis=2).astype(jnp.bfloat16)
    pooled_local = pooled_local.reshape(sample_count, col_piece)
    pooled = lax.all_to_all(pooled_local, "dp", split_axis=0, concat_axis=1, tiled=True)
    upstream = cotangent.astype(jnp.float32)
    grad_gate = (upstream * pooled.astype(jnp.float32)).astype(jnp.bfloat16)
    down_full, up_full = (
        lax.all_gather(cross_down, "fsdp", axis=0, tiled=True),
        lax.all_gather(cross_up, "fsdp", axis=1, tiled=True),
    )
    low_rank = jnp.dot(pooled, down_full, preferred_element_type=jnp.float32).astype(jnp.bfloat16)
    gate_value = jnp.dot(low_rank, up_full, preferred_element_type=jnp.float32) + cross_bias
    grad_low = lax.dot_general(
        grad_gate, up_full, (((1,), (1,)), ((), ())), preferred_element_type=jnp.float32
    ).astype(jnp.bfloat16)
    back_term = lax.dot_general(
        grad_low, down_full, (((1,), (1,)), ((), ())), preferred_element_type=jnp.float32
    )
    grad_pooled = (upstream * (gate_value + 1.0) + back_term).astype(jnp.bfloat16)
    grad_local = lax.all_to_all(grad_pooled, "dp", split_axis=1, concat_axis=0, tiled=True)
    partial_value = scatter_rows(
        vocab_rows, got_ids, grad_local, local_tables, slot_count, embed_width, 0
    )
    return lax.psum_scatter(partial_value, "fsdp", scatter_dimension=0, tiled=True)


def solution(mesh):
    placed = (
        P(("dp", "fsdp"), None, None),
        P(("dp", "fsdp"), None),
        P(None, "dp"),
        P("fsdp", None),
        P(None, "fsdp"),
        P(),
        P(("dp", "fsdp"), None),
    )
    return jax.shard_map(
        on_device, mesh=mesh, in_specs=placed, out_specs=P("fsdp", "dp"), check_vma=False
    )
```

profile of v0, /device:TPU:1, one launch (start us, length us, event | category | flops | bytes accessed | tf_op | source)
XLA Modules:
  0.0 684.6 jit_solution(626548155860651845)
XLA Ops:
  6.5 0.0 copy-start
  6.5 0.0 copy-start.2
  6.5 0.0 copy-start.4
  6.5 0.0 all-gather.3.cloned.1.call-start
  6.5 0.7 all-gather.3.cloned.1.call-update
  7.3 0.0 all-gather.5.cloned.1.call-start
  7.3 0.7 all-gather.5.cloned.1.call-update
  8.0 0.0 copy-done.2
  8.0 0.0 copy-done.4
  8.1 18.7 %all_to_all.45 = s32[128,64,4]{0,2,1:T(4,128)S(1)} all-to-all(s32[128,64,4]{0,2,1:T(4,128)S(1)} %fusion.24), channel_id=1, replica_groups=mesh['dp'=64,'fsdp'=4] {'dp'}, dimensions={1} | all-to-all | bytes 262144 | tf_op jit(solution)/shard_map/all_to_all | solution.py:29
  26.8 2.7 copy.10
  29.5 5.1 reshape.183
  34.5 0.1 compare_and_fusion
  34.6 1.7 copy.9
  36.4 0.0 copy-done
  36.4 114.2 %gather_fusion = bf16[32768,128]{1,0:T(8,128)(2,1)} fusion(bf16[8192,128]{1,0:T(8,128)(2,1)S(1)} %copy-done, s32[32768]{0:T(1024)S(1)} %broadcast_clamp_fusion), kind=kCustom, calls=%fused_computation | custom fusion | bytes 16908288 | tf_op jit(solution)/shard_map/jit(_take)/gather | solution.py:33
  150.6 47.3 %select_reduce_fusion = bf16[8192,128]{1,0:T(8,128)(2,1)} fusion(bf16[8192,1,4,128]{3,2,0,1:T(4,128)(2,1)} %bitcast.54, pred[8192,4]{1,0:T(8,128)(4,1)S(1)} %copy.9), kind=kLoop, calls=%fused_computation.7 | loop fusion | flops 7340032 | bytes 10518528 | tf_op jit(solution)/shard_map/reduce_sum | solution.py:34
  197.9 4.6 all-to-all-start.1
  202.5 0.0 copy-start.3
  202.5 2.7 copy.8
  205.1 6.1 reshape.176
  211.3 87.0 %all-to-all-done.1 = bf16[64,128,128]{2,1,0:T(8,128)(2,1)S(1)} async-done(((bf16[64,128,128]{2,1,0:T(8,128)(2,1)}), bf16[64,128,128]{2,1,0:T(8,128)(2,1)S(1)}, u32[]{:S(2)}, u32[]{:S(2)}) %all-to-all-start.1) | async-done | bytes 2097184 | tf_op jit(solution)/shard_map/all_to_all | solution.py:36
  298.3 0.0 all-gather.3.cloned.1.call-done
  298.3 48.7 %all-gather.5.cloned.1.call-done = bf16[512,8192]{1,0:T(8,128)(2,1)} async-done(((bf16[512,2048]{1,0:T(8,128)(2,1)}), bf16[512,8192]{1,0:T(8,128)(2,1)}) %all-gather.5.cloned.1.call-update) | async-done | bytes 8388624 | tf_op jit(solution)/shard_map/all_gather | solution.py:41
  347.0 0.0 copy-done.3
  347.0 11.1 %fusion.1 = f32[128,8192]{1,0:T(8,128)} fusion(bf16[512,8192]{1,0:T(8,128)(2,1)} %all-gather.5.cloned.1.call-done, bf16[128,8192]{1,0:T(8,128)(2,1)} %param.13, f32[8192]{0:T(1024)S(1)} %copy-done.3, bf16[8192,512]{1,0:T(8,128)(2,1)} %all-gather.3.cloned.1.call-done, bf16[64,128,128]{2,1,0:T(8,128)(2,1)S(1)} %all-to-all-done.1), kind=kOutput, calls=%fused_computation.5 | convolution fusion | flops 2151743488 | bytes 25198592 | tf_op jit(solution)/shard_map/dot_general | solution.py:44
  358.1 15.4 %fusion.13 = bf16[16,64,8,128]{3,2,1,0:T(8,128)(2,1)} fusion(f32[128,8192]{1,0:T(8,128)} %fusion.1, bf16[8192,512]{1,0:T(8,128)(2,1)} %all-gather.3.cloned.1.call-done, bf16[512,8192]{1,0:T(8,128)(2,1)} %all-gather.5.cloned.1.call-done, bf16[128,8192]{1,0:T(8,128)(2,1)} %param.13, bf16[64,128,128]{2,1,0:T(8,128)(2,1)S(1)} %all-to-all-done.1), kind=kOutput, calls=%fused_computation.19 | convolution fusion | flops 2153840640 | bytes 27262976 | tf_op jit(solution)/shard_map/dot_general | solution.py:48
  373.5 3.5 copy.32
  377.0 7.9 %all-to-all-start.2 = ((bf16[128,64,128]{2,0,1:T(8,128)(2,1)}), bf16[128,64,128]{2,0,1:T(8,128)(2,1)S(1)}, u32[]{:S(2)}, u32[]{:S(2)}) async-start(bf16[128,64,128]{2,0,1:T(8,128)(2,1)} %bitcast.57), calls=%async_computation.2 | async-start | bytes 4194304 | tf_op jit(solution)/shard_map/all_to_all | solution.py:52
  384.9 0.3 reduce-scatter.2.cloned.1.call-start
  385.2 0.2 compare_select_fusion
  385.4 28.5 %all-to-all-done.2 = bf16[128,64,128]{2,0,1:T(8,128)(2,1)S(1)} async-done(((bf16[128,64,128]{2,0,1:T(8,128)(2,1)}), bf16[128,64,128]{2,0,1:T(8,128)(2,1)S(1)}, u32[]{:S(2)}, u32[]{:S(2)}) %all-to-all-start.2) | async-done | bytes 2097184 | tf_op jit(solution)/shard_map/all_to_all | solution.py:52
  414.0 0.5 convert_element_type.44
  414.5 7.4 %broadcast_in_dim.31 = f32[8192,1,4,128]{3,2,0,1:T(4,128)} broadcast(f32[8192,128]{1,0:T(8,128)S(1)} %bitcast.56), dimensions={0,3} | broadcast | bytes 20971520 | tf_op jit(solution)/shard_map/broadcast_in_dim | solution.py:14
  421.9 0.0 copy-start.1
  421.9 176.5 %scatter_custom_fusion = f32[8192,128]{1,0:T(8,128)} fusion(s32[32768]{0:T(1024)S(1)} %bitcast.60, f32[32768,128]{1,0:T(8,128)} %bitcast.55, f32[]{:T(128)} %constant.7.clone.1), kind=kCustom, calls=%fused_computation.15 | custom fusion | flops 4194304 | bytes 4194816 | tf_op jit(solution)/shard_map/scatter-add | solution.py:16
  598.4 0.0 reduce-scatter.2.cloned.1.call-update
  598.5 79.6 %reduce-scatter.2.cloned.1.call-done = f32[2048,128]{1,0:T(8,128)} async-done(((f32[8192,128]{1,0:T(8,128)}), f32[2048,128]{1,0:T(8,128)}) %reduce-scatter.2.cloned.1.call-update) | async-done | bytes 1048592 | tf_op jit(solution)/shard_map/reduce_scatter | solution.py:56
  678.0 0.0 copy-done.1
  (3 shorter events, 0.1 us)
Async XLA Ops:
  6.5 29.9 %copy-start = (bf16[8192,128]{1,0:T(8,128)(2,1)S(1)}, bf16[8192,128]{1,0:T(8,128)(2,1)}, u32[]{:S(2)}) copy-start(bf16[8192,128]{1,0:T(8,128)(2,1)} %param.9) | copy-start | bytes 6291460
  6.5 1.5 copy-start.2
  6.5 1.5 copy-start.4
  6.5 291.8 %all-gather.3.cloned.1.call-start = ((), (), s32[]{:S(2)}) async-start(), calls=%async_computation.4 | async-start | bytes 10485760 | tf_op jit(solution)/shard_map/all_gather | solution.py:40
  7.3 339.7 %all-gather.5.cloned.1.call-start = ((), (), s32[]{:S(2)}) async-start(), calls=%async_computation.5 | async-start | bytes 10485760 | tf_op jit(solution)/shard_map/all_gather | solution.py:41
  197.9 100.4 %all-to-all-start.1 = ((bf16[64,128,128]{2,1,0:T(8,128)(2,1)}), bf16[64,128,128]{2,1,0:T(8,128)(2,1)S(1)}, u32[]{:S(2)}, u32[]{:S(2)}) async-start(bf16[64,128,128]{2,1,0:T(8,128)(2,1)} %bitcast.58), calls=%async_computation.1 | async-start | bytes 4194304 | tf_op jit(solution)/shard_map/all_to_all | solution.py:36
  202.5 144.5 %copy-start.3 = (f32[8192]{0:T(1024)S(1)}, f32[8192]{0:T(1024)}, u32[]{:S(2)}) copy-start(f32[8192]{0:T(1024)} %param.12) | copy-start | bytes 98308
  377.0 37.0 %all-to-all-start.2 = ((bf16[128,64,128]{2,0,1:T(8,128)(2,1)}), bf16[128,64,128]{2,0,1:T(8,128)(2,1)S(1)}, u32[]{:S(2)}, u32[]{:S(2)}) async-start(bf16[128,64,128]{2,0,1:T(8,128)(2,1)} %bitcast.57), calls=%async_computation.2 | async-start | bytes 4194304 | tf_op jit(solution)/shard_map/all_to_all | solution.py:52
  384.9 293.1 %reduce-scatter.2.cloned.1.call-start = ((), (), s32[]{:S(2)}) async-start(), calls=%async_computation.6 | async-start | bytes 5242880 | tf_op jit(solution)/shard_map/reduce_scatter | solution.py:56
  421.9 256.1 %copy-start.1 = (bf16[8192,128]{1,0:T(8,128)(2,1)S(1)}, bf16[8192,128]{1,0:T(8,128)(2,1)}, u32[]{:S(2)}) copy-start(bf16[8192,128]{1,0:T(8,128)(2,1)} %param.9) | copy-start | bytes 6291460
Sparse Core Ops, SparseCore 0:
  9.2 159.0 all-gather.2
  170.1 176.8 all-gather.4
  598.6 79.4 reduce-scatter.1
where the time goes:
time: 685 us
  waiting for transfers between devices  245 us (36%)
  other arithmetic  225 us (33%)
  local copies, waits for them, and re-layouts  143 us (21%)
  matrix products  26.5 us (4%)
  blocking collectives  18.7 us (3%)
  between operations  13.2 us (2%)
  starting transfers between devices  12.8 us (2%)
    scatter-add x1, other arithmetic, scatter_rows(): target.at[flat_rows.reshape(-1)]  177 us
    gather x1, local copies, waits for them, and re-layouts, on_device(): picked = jnp.take(emb_table, flat_ids, axis=0, mode='fill', fill_value=0)  114 us
    all_to_all x1, waiting for transfers between devices, on_device(): lax.all_to_all(pooled_local, 'dp', split_axis=0, concat_axis=1, tiled=True)  87 us
    reduce_scatter x1, waiting for transfers between devices, on_device(): lax.psum_scatter(partial_value, 'fsdp', scatter_dimension=0, tiled=True)  79.6 us
    all_gather x1, waiting for transfers between devices, on_device(): lax.all_gather(cross_up, 'fsdp', axis=1, tiled=True)  48.7 us
    reduce_sum x1, other arithmetic, on_device(): jnp.sum(picked.astype(jnp.float32), axis=2).astype(jnp.bfloat16)  47.3 us
    all_to_all x1, waiting for transfers between devices, on_device(): lax.all_to_all(grad_pooled, 'dp', split_axis=1, concat_axis=0, tiled=True)  28.5 us
    all_to_all x1, blocking collectives, on_device(): lax.all_to_all(send_ids, 'dp', split_axis=1, concat_axis=0, tiled=True)  18.7 us
  transfers between devices with their start and end apart: 5, of which 4 were waited for; matrix products, arithmetic and copies ran while one was open for 26% of the time, Pallas kernels for 0%

commit v1 on v0

--- a/solution.py
+++ b/solution.py
@@ -38,7 +38,9 @@
     grad_gate = (upstream * pooled.astype(jnp.float32)).astype(jnp.bfloat16)
     down_full, up_full = (
         lax.all_gather(cross_down, "fsdp", axis=0, tiled=True),
-        lax.all_gather(cross_up, "fsdp", axis=1, tiled=True),
+        jnp.concatenate(
+            lax.all_to_all(jnp.stack([cross_up] * lax.axis_size("fsdp")), "fsdp", 0, 0), axis=1
+        ),
     )
     low_rank = jnp.dot(pooled, down_full, preferred_element_type=jnp.float32).astype(jnp.bfloat16)
     gate_value = jnp.dot(low_rank, up_full, preferred_element_type=jnp.float32) + cross_bias

time: 685 us -> 900 us (1.31)
  waiting for transfers between devices: 245 us -> 446 us
  local copies, waits for them, and re-layouts: 143 us -> 153 us
    all_to_all x0 -> x1, waiting for transfers between devices: none -> 287 us  [on_device(): lax.all_to_all(jnp.stack([cross_up] * lax.axis_size('fsdp')), 'fsdp', 0, 0)]
    all_to_all x1, waiting for transfers between devices: 87 us -> 25.2 us  [on_device(): lax.all_to_all(pooled_local, 'dp', split_axis=0, concat_axis=1, tiled=True)]
    all_gather x1 -> x0, waiting for transfers between devices: 48.7 us -> none  [on_device(): lax.all_gather(cross_up, 'fsdp', axis=1, tiled=True)]
    all_gather x1, waiting for transfers between devices: 0.01 us -> 24.1 us  [on_device(): lax.all_gather(cross_down, 'fsdp', axis=0, tiled=True)]
  transfers between devices with their start and end apart: 5 -> 5, of which waited for: 4 -> 5; matrix products, arithmetic and copies ran while one was open for 26% -> 1% of each run, Pallas kernels for 0% -> 0%
where the time goes in v1:
time: 900 us; the launch traced here: 899 us
  waiting for transfers between devices  446 us (50%)
  other arithmetic  226 us (25%)
  local copies, waits for them, and re-layouts  153 us (17%)
  matrix products  25.2 us (3%)
  blocking collectives  18.7 us (2%)
  starting transfers between devices  16.7 us (2%)
  between operations  13.5 us (2%)
    all_to_all x1, waiting for transfers between devices, on_device(): lax.all_to_all(jnp.stack([cross_up] * lax.axis_size('fsdp')), 'fsdp', 0, 0)  287 us
    scatter-add x1, other arithmetic, scatter_rows(): target.at[flat_rows.reshape(-1)]  177 us
    gather x1, local copies, waits for them, and re-layouts, on_device(): picked = jnp.take(emb_table, flat_ids, axis=0, mode='fill', fill_value=0)  115 us
    reduce_scatter x1, waiting for transfers between devices, on_device(): lax.psum_scatter(partial_value, 'fsdp', scatter_dimension=0, tiled=True)  80.3 us
    reduce_sum x1, other arithmetic, on_device(): jnp.sum(picked.astype(jnp.float32), axis=2).astype(jnp.bfloat16)  47.3 us
    all_to_all x1, waiting for transfers between devices, on_device(): lax.all_to_all(grad_pooled, 'dp', split_axis=1, concat_axis=0, tiled=True)  28.6 us
    all_to_all x1, waiting for transfers between devices, on_device(): lax.all_to_all(pooled_local, 'dp', split_axis=0, concat_axis=1, tiled=True)  25.2 us
    all_gather x1, waiting for transfers between devices, on_device(): lax.all_gather(cross_down, 'fsdp', axis=0, tiled=True)  24.1 us
  transfers between devices with their start and end apart: 5, of which 5 were waited for; matrix products, arithmetic and copies ran while one was open for 1% of the time, Pallas kernels for 0%

profile of v1, /device:TPU:1, one launch (start us, length us, event | category | flops | bytes accessed | tf_op | source)
XLA Modules:
  0.0 899.2 jit_solution(2645602364037097324)
XLA Ops:
  6.5 0.0 copy-start
  6.5 1.1 fusion.24
  7.6 18.7 %all_to_all.50 = s32[128,64,4]{0,2,1:T(4,128)S(1)} all-to-all(s32[128,64,4]{0,2,1:T(4,128)S(1)} %fusion.24), channel_id=1, replica_groups=mesh['dp'=64,'fsdp'=4] {'dp'}, dimensions={1} | all-to-all | bytes 262144 | tf_op jit(solution)/shard_map/all_to_all | solution.py:29
  26.4 2.6 copy.10
  29.0 4.9 reshape.193
  33.9 0.1 compare_and_fusion
  34.0 1.7 copy.9
  35.7 0.0 copy-done
  35.7 115.0 %gather_fusion = bf16[32768,128]{1,0:T(8,128)(2,1)} fusion(bf16[8192,128]{1,0:T(8,128)(2,1)S(1)} %copy-done, s32[32768]{0:T(1024)S(1)} %broadcast_clamp_fusion), kind=kCustom, calls=%fused_computation | custom fusion | bytes 16908288 | tf_op jit(solution)/shard_map/jit(_take)/gather | solution.py:33
  150.7 47.3 %select_reduce_fusion = bf16[8192,128]{1,0:T(8,128)(2,1)} fusion(bf16[8192,1,4,128]{3,2,0,1:T(4,128)(2,1)} %bitcast.57, pred[8192,4]{1,0:T(8,128)(4,1)S(1)} %copy.9), kind=kLoop, calls=%fused_computation.7 | loop fusion | flops 7340032 | bytes 10518528 | tf_op jit(solution)/shard_map/reduce_sum | solution.py:34
  198.0 4.5 all-to-all-start.1
  202.6 3.9 copy.12
  206.5 25.2 %all-to-all-done.1 = bf16[64,128,128]{2,1,0:T(8,128)(2,1)S(1)} async-done(((bf16[64,128,128]{2,1,0:T(8,128)(2,1)}), bf16[64,128,128]{2,1,0:T(8,128)(2,1)S(1)}, u32[]{:S(2)}, u32[]{:S(2)}) %all-to-all-start.1) | async-done | bytes 2097184 | tf_op jit(solution)/shard_map/all_to_all | solution.py:36
  231.7 5.5 stack.2
  237.2 7.3 all-to-all-start.2
  244.5 0.0 all-gather.2.cloned.1.call-start
  244.5 0.7 all-gather.2.cloned.1.call-update
  245.2 0.0 copy-start.2
  245.3 2.7 copy.8
  247.9 6.1 reshape.184
  254.0 287.0 %all-to-all-done.2 = bf16[4,512,2048]{1,2,0:T(8,128)(2,1)} async-done(((bf16[4,512,2048]{1,2,0:T(8,128)(2,1)}), bf16[4,512,2048]{1,2,0:T(8,128)(2,1)}, u32[]{:S(2)}, u32[]{:S(2)}) %all-to-all-start.2) | async-done | bytes 8388640 | tf_op jit(solution)/shard_map/all_to_all | solution.py:42
  541.0 24.1 %all-gather.2.cloned.1.call-done = bf16[8192,512]{1,0:T(8,128)(2,1)} async-done(((bf16[2048,512]{1,0:T(8,128)(2,1)}), bf16[8192,512]{1,0:T(8,128)(2,1)}) %all-gather.2.cloned.1.call-update) | async-done | bytes 8388624 | tf_op jit(solution)/shard_map/all_gather | solution.py:40
  565.1 0.0 copy-done.2
  565.1 12.3 %fusion.1 = f32[128,8192]{1,0:T(8,128)} fusion(bf16[512,8192]{0,1:T(8,128)(2,1)} %bitcast.10, bf16[128,8192]{1,0:T(8,128)(2,1)} %param.13, f32[8192]{0:T(1024)S(1)} %copy-done.2, bf16[8192,512]{1,0:T(8,128)(2,1)} %all-gather.2.cloned.1.call-done, bf16[64,128,128]{2,1,0:T(8,128)(2,1)S(1)} %all-to-all-done.1), kind=kOutput, calls=%fused_computation.5 | convolution fusion | flops 2151743488 | bytes 25198592 | tf_op jit(solution)/shard_map/dot_general | solution.py:46
  577.4 12.9 %fusion.13 = bf16[16,64,8,128]{3,2,1,0:T(8,128)(2,1)} fusion(f32[128,8192]{1,0:T(8,128)} %fusion.1, bf16[8192,512]{1,0:T(8,128)(2,1)} %all-gather.2.cloned.1.call-done, bf16[512,8192]{0,1:T(8,128)(2,1)} %bitcast.10, bf16[128,8192]{1,0:T(8,128)(2,1)} %param.13, bf16[64,128,128]{2,1,0:T(8,128)(2,1)S(1)} %all-to-all-done.1), kind=kOutput, calls=%fused_computation.19 | convolution fusion | flops 2153840640 | bytes 27262976 | tf_op jit(solution)/shard_map/dot_general | solution.py:50
  590.3 3.5 copy.33
  593.8 4.6 all-to-all-start.3
  598.4 0.3 reduce-scatter.2.cloned.1.call-start
  598.7 0.2 compare_select_fusion
  598.9 28.6 %all-to-all-done.3 = bf16[128,64,128]{2,0,1:T(8,128)(2,1)S(1)} async-done(((bf16[128,64,128]{2,0,1:T(8,128)(2,1)}), bf16[128,64,128]{2,0,1:T(8,128)(2,1)S(1)}, u32[]{:S(2)}, u32[]{:S(2)}) %all-to-all-start.3) | async-done | bytes 2097184 | tf_op jit(solution)/shard_map/all_to_all | solution.py:54
  627.6 0.5 convert_element_type.44
  628.1 7.4 broadcast_in_dim.31
  635.5 0.0 copy-start.1
  635.5 176.5 %scatter_custom_fusion = f32[8192,128]{1,0:T(8,128)} fusion(s32[32768]{0:T(1024)S(1)} %bitcast.63, f32[32768,128]{1,0:T(8,128)} %bitcast.58, f32[]{:T(128)} %constant.7.clone.1), kind=kCustom, calls=%fused_computation.15 | custom fusion | flops 4194304 | bytes 4194816 | tf_op jit(solution)/shard_map/scatter-add | solution.py:16
  812.1 0.0 reduce-scatter.2.cloned.1.call-update
  812.1 80.3 %reduce-scatter.2.cloned.1.call-done = f32[2048,128]{1,0:T(8,128)} async-done(((f32[8192,128]{1,0:T(8,128)}), f32[2048,128]{1,0:T(8,128)}) %reduce-scatter.2.cloned.1.call-update) | async-done | bytes 1048592 | tf_op jit(solution)/shard_map/reduce_scatter | solution.py:58
  892.4 0.0 copy-done.1
  (2 shorter events, 0.1 us)
Async XLA Ops:
  6.5 29.2 %copy-start = (bf16[8192,128]{1,0:T(8,128)(2,1)S(1)}, bf16[8192,128]{1,0:T(8,128)(2,1)}, u32[]{:S(2)}) copy-start(bf16[8192,128]{1,0:T(8,128)(2,1)} %param.9) | copy-start | bytes 6291460
  198.0 33.7 %all-to-all-start.1 = ((bf16[64,128,128]{2,1,0:T(8,128)(2,1)}), bf16[64,128,128]{2,1,0:T(8,128)(2,1)S(1)}, u32[]{:S(2)}, u32[]{:S(2)}) async-start(bf16[64,128,128]{2,1,0:T(8,128)(2,1)} %bitcast.61), calls=%async_computation.1 | async-start | bytes 4194304 | tf_op jit(solution)/shard_map/all_to_all | solution.py:36
  237.2 303.8 %all-to-all-start.2 = ((bf16[4,512,2048]{1,2,0:T(8,128)(2,1)}), bf16[4,512,2048]{1,2,0:T(8,128)(2,1)}, u32[]{:S(2)}, u32[]{:S(2)}) async-start(bf16[4,512,2048]{1,2,0:T(8,128)(2,1)} %stack.2), calls=%async_computation.2 | async-start | bytes 16777216 | tf_op jit(solution)/shard_map/all_to_all | solution.py:42
  244.5 320.6 %all-gather.2.cloned.1.call-start = ((), (), s32[]{:S(2)}) async-start(), calls=%async_computation.5 | async-start | bytes 10485760 | tf_op jit(solution)/shard_map/all_gather | solution.py:40
  245.2 319.9 %copy-start.2 = (f32[8192]{0:T(1024)S(1)}, f32[8192]{0:T(1024)}, u32[]{:S(2)}) copy-start(f32[8192]{0:T(1024)} %param.12) | copy-start | bytes 98308
  593.8 33.8 %all-to-all-start.3 = ((bf16[128,64,128]{2,0,1:T(8,128)(2,1)}), bf16[128,64,128]{2,0,1:T(8,128)(2,1)S(1)}, u32[]{:S(2)}, u32[]{:S(2)}) async-start(bf16[128,64,128]{2,0,1:T(8,128)(2,1)} %bitcast.60), calls=%async_computation.3 | async-start | bytes 4194304 | tf_op jit(solution)/shard_map/all_to_all | solution.py:54
  598.4 294.0 %reduce-scatter.2.cloned.1.call-start = ((), (), s32[]{:S(2)}) async-start(), calls=%async_computation.6 | async-start | bytes 5242880 | tf_op jit(solution)/shard_map/reduce_scatter | solution.py:58
  635.5 256.8 %copy-start.1 = (bf16[8192,128]{1,0:T(8,128)(2,1)S(1)}, bf16[8192,128]{1,0:T(8,128)(2,1)}, u32[]{:S(2)}) copy-start(bf16[8192,128]{1,0:T(8,128)(2,1)} %param.9) | copy-start | bytes 6291460
Sparse Core Ops, SparseCore 0:
  247.1 317.8 all-gather.1
  812.2 80.1 reduce-scatter.1
